TPU v7x, 128 devices: a whole 4x4x4 slice. The times are simulated.
128 devices in a mesh: inline: 16 (over z, x), crosslin: 8 (over y, core).
Axes of the slice: x: 4, y: 4, z: 4, core: 2. Of those that a mesh axis runs over, the one named last changes fastest.
Arguments:
- grid_feat: bfloat16 [262144, 512], P(('inline', 'crosslin')), may hold values from -68 to 68
- cotangent: bfloat16 [262144, 512], P(('inline', 'crosslin')), may hold values from -6 to 6
- trace_feat: bfloat16 [16384, 512], P(('inline', 'crosslin')), may hold values from -6 to 6
- trace_dest: int32 [16384, 2], P(('inline', 'crosslin')), may hold values from 0 to 127, all different within a row; in each aligned block of 128 rows (0 to 127, 128 to 255, ...) at most 4 rows name the same one
- query_weight: bfloat16 [512, 512], replicated, may hold values from -0.25 to 0.25
- key_weight: bfloat16 [512, 512], replicated, may hold values from -0.25 to 0.25
- value_weight: bfloat16 [512, 512], replicated, may hold values from -0.25 to 0.25
- output_weight: bfloat16 [512, 512], replicated, may hold values from -0.25 to 0.25
Outputs:
- grad_grid: bfloat16 [262144, 512], P(('inline', 'crosslin'))
- grad_trace: float32 [16384, 512], P(('inline', 'crosslin'))
- grad_query: float32 [512, 512], replicated
- grad_key: float32 [512, 512], replicated
- grad_value: float32 [512, 512], replicated
- grad_output: float32 [512, 512], replicated
Inputs may be any that keep to these rules, and one draw needn't show every extreme that they name: `trace_dest`: in the 128 rows of one device no tile is named by more than 4 rows, a bound that some block reaches; a row names 2 different tiles; every tile is named by some row.
All inputs are finite; a program needn't handle non-finite values.
Results may differ from a plain program's by a relative error of at most 0.013.
The roundings to bfloat16 on the way count: a program that leaves them out, or rounds other values in their place, can miss the bound.
Values may be sent and summed in bfloat16 or wider, within the bound.
No kernel may reach another device: no remote copies, remote signals or barrier semaphores. Data moves between devices by JAX's collectives and lax.ppermute only.
A program may use at most 64 MiB of HBM per device.

v0:
```python
import jax
import jax.numpy as jnp
from jax import lax
from jax.sharding import PartitionSpec as P

HEADS = 8
TOP = 2


def slot_table(targets, tile_count, capacity):
    tile_ids = jnp.arange(tile_count, dtype=jnp.int32)
    named = jnp.any(targets[:, :, None] == tile_ids[None, None, :], axis=1)
    position = jnp.cumsum(named.astype(jnp.int32), axis=0) - 1
    places = jnp.arange(capacity, dtype=jnp.int32)
    chosen = named.T[:, None, :] & (position.T[:, None, :] == places[None, :, None])
    return (chosen, jnp.sum(named.astype(jnp.int32), axis=0))


def tile_grad(grid_rows, upstream, query_weight, output_weight, key_tile, value_tile, live_slots):
    model_width = grid_rows.shape[1]
    head_size = model_width // HEADS
    factor = head_size ** (-0.5)
    queries = jnp.dot(grid_rows, query_weight, preferred_element_type=jnp.float32).astype(
        jnp.bfloat16
    )
    out_grad = jnp.dot(upstream, output_weight.T, preferred_element_type=jnp.float32).astype(
        jnp.bfloat16
    )

    def one_head(head_index):
        offset = head_index * head_size
        query_head = lax.dynamic_slice_in_dim(queries, offset, head_size, 1)
        key_head = lax.dynamic_slice_in_dim(key_tile, offset, head_size, 1)
        value_head = lax.dynamic_slice_in_dim(value_tile, offset, head_size, 1)
        grad_head = lax.dynamic_slice_in_dim(out_grad, offset, head_size, 1)
        scores = jnp.dot(query_head, key_head.T, preferred_element_type=jnp.float32) * factor
        scores = jnp.where(live_slots[None, :], scores, -1e30)
        row_peak = jnp.max(scores, axis=1, keepdims=True)
        raised = jnp.exp(scores - row_peak)
        attention = raised / jnp.sum(raised, axis=1, keepdims=True)
        prob_half = attention.astype(jnp.bfloat16)
        head_out = jnp.dot(prob_half, value_head, preferred_element_type=jnp.float32).astype(
            jnp.bfloat16
        )
        prob_grad = jnp.dot(grad_head, value_head.T, preferred_element_type=jnp.float32)
        correction = jnp.sum(attention * prob_grad, axis=1, keepdims=True)
        score_grad = (attention * (prob_grad - correction) * factor).astype(jnp.bfloat16)
        query_grad = jnp.dot(score_grad, key_head, preferred_element_type=jnp.float32).astype(
            jnp.bfloat16
        )
        key_grad = jnp.dot(score_grad.T, query_head, preferred_element_type=jnp.float32).astype(
            jnp.bfloat16
        )
        value_grad = jnp.dot(prob_half.T, grad_head, preferred_element_type=jnp.float32).astype(
            jnp.bfloat16
        )
        return (head_out, query_grad, key_grad, value_grad)

    def join_heads(stacked):
        return jnp.transpose(stacked, (1, 0, 2)).reshape(stacked.shape[1], model_width)

    stacked = lax.map(one_head, jnp.arange(HEADS, dtype=jnp.int32))
    attn_out, query_grad, key_grad, value_grad = [
        join_heads(stacked_part) for stacked_part in stacked
    ]
    part_output = jnp.dot(attn_out.T, upstream, preferred_element_type=jnp.float32)
    grad_grid = jnp.dot(query_grad, query_weight.T, preferred_element_type=jnp.float32).astype(
        jnp.bfloat16
    )
    part_query = jnp.dot(grid_rows.T, query_grad, preferred_element_type=jnp.float32)
    return (grad_grid, key_grad, value_grad, part_output, part_query)


def send_slots(outgoing):
    arrived = lax.all_to_all(
        outgoing, ("inline", "crosslin"), split_axis=0, concat_axis=0, tiled=True
    )
    return arrived


def send_back(returned):
    result_rows = lax.all_to_all(
        returned, ("inline", "crosslin"), split_axis=0, concat_axis=0, tiled=True
    )
    return result_rows


def on_device(
    grid_feat,
    cotangent,
    trace_feat,
    trace_dest,
    query_weight,
    key_weight,
    value_weight,
    output_weight,
):
    tile_count = lax.axis_size("inline") * lax.axis_size("crosslin")
    trace_rows = trace_feat.shape[0]
    model_width = trace_feat.shape[1]
    capacity = 2 * trace_rows * TOP // tile_count
    chosen, counts = slot_table(trace_dest, tile_count, capacity)
    picker = chosen.astype(jnp.bfloat16)
    key_rows = jnp.dot(trace_feat, key_weight, preferred_element_type=jnp.float32).astype(
        jnp.bfloat16
    )
    value_rows = jnp.dot(trace_feat, value_weight, preferred_element_type=jnp.float32).astype(
        jnp.bfloat16
    )
    flag = jnp.ones((trace_rows, 128), jnp.bfloat16)
    packed = jnp.concatenate([key_rows, value_rows, trace_feat, flag], axis=1)
    outgoing = jnp.einsum("tjr,rd->tjd", picker, packed, preferred_element_type=jnp.float32).astype(
        jnp.bfloat16
    )
    arrived = send_slots(outgoing)
    arrived = arrived.reshape(tile_count * capacity, packed.shape[1])
    key_tile = arrived[:, :model_width]
    value_tile = arrived[:, model_width : 2 * model_width]
    feat_tile = arrived[:, 2 * model_width : 3 * model_width]
    live_slots = arrived[:, 3 * model_width] > 0.5
    grad_grid, key_grad, value_grad, part_output, part_query = tile_grad(
        grid_feat, cotangent, query_weight, output_weight, key_tile, value_tile, live_slots
    )
    part_key = jnp.dot(feat_tile.T, key_grad, preferred_element_type=jnp.float32)
    part_value = jnp.dot(feat_tile.T, value_grad, preferred_element_type=jnp.float32)
    grad_query, grad_key, grad_value, grad_output = lax.psum(
        (part_query, part_key, part_value, part_output), ("inline", "crosslin")
    )
    slot_trace = jnp.dot(key_grad, key_weight.T, preferred_element_type=jnp.float32)
    slot_trace = slot_trace + jnp.dot(
        value_grad, value_weight.T, preferred_element_type=jnp.float32
    )
    slot_trace = slot_trace.astype(jnp.bfloat16).reshape(tile_count, capacity, model_width)
    returned = send_back(slot_trace)
    grad_trace = jnp.einsum("tjr,tje->re", picker, returned, preferred_element_type=jnp.float32)
    return (grad_grid, grad_trace, grad_query, grad_key, grad_value, grad_output)


def solution(mesh):
    in_specs = (
        P(("inline", "crosslin"), None),
        P(("inline", "crosslin"), None),
        P(("inline", "crosslin"), None),
        P(("inline", "crosslin"), None),
        P(),
        P(),
        P(),
        P(),
    )
    out_specs = (
        P(("inline", "crosslin"), None),
        P(("inline", "crosslin"), None),
        P(),
        P(),
        P(),
        P(),
    )
    return jax.shard_map(
        on_device, mesh=mesh, in_specs=in_specs, out_specs=out_specs, check_vma=False
    )
```

profile of v0, /device:TPU:1, one launch (start us, length us, event | category | flops | bytes accessed | tf_op | source)
XLA Modules:
  0.0 360.5 jit_solution(8484255130443011278)
XLA Ops:
  8.3 1.3 convolution_convert_fusion.8
  9.7 1.3 convolution_convert_fusion.9
  11.0 1.6 convolution_convert_fusion.7
  12.6 2.5 copy.29
  15.1 11.9 %all-to-all-start = ((bf16[128,4,1664]{2,1,0:T(4,128)(2,1)}), bf16[128,4,1664]{2,1,0:T(4,128)(2,1)}, u32[]{:S(2)}, u32[]{:S(2)}) async-start(bf16[128,4,1664]{2,1,0:T(4,128)(2,1)} %copy.29), calls=%async_computation | async-start | bytes 3407872 | tf_op jit(solution)/shard_map/all_to_all | solution.py:75
  27.1 4.2 %convolution_convert_fusion.5 = bf16[2048,512]{1,0:T(8,128)(2,1)} fusion(bf16[2048,512]{1,0:T(8,128)(2,1)} %param.11, bf16[512,512]{1,0:T(8,128)(2,1)S(1)} %copy-done.9), kind=kOutput, calls=%fused_computation.38 | convolution fusion | flops 1074790400 | bytes 4718592 | tf_op jit(solution)/shard_map/dot_general | solution.py:26
  31.4 2.6 convolution_convert_fusion.6
  34.0 18.7 %all-to-all-done = bf16[128,4,1664]{2,1,0:T(4,128)(2,1)} async-done(((bf16[128,4,1664]{2,1,0:T(4,128)(2,1)}), bf16[128,4,1664]{2,1,0:T(4,128)(2,1)}, u32[]{:S(2)}, u32[]{:S(2)}) %all-to-all-start) | async-done | bytes 1703968 | tf_op jit(solution)/shard_map/all_to_all | solution.py:75
  52.7 3.8 %reshape.41 = bf16[512,1664]{1,0:T(8,128)(2,1)} reshape(bf16[128,4,1664]{2,1,0:T(4,128)(2,1)} %all-to-all-done) | data formatting | bytes 3407872 | tf_op jit(solution)/shard_map/reshape | solution.py:116
  56.5 2.1 fusion.52
  59.7 121.5 %while.16 = (s32[]{:T(128)}, bf16[8,2048,64]{1,2,0:T(8,128)(2,1)}, bf16[8,2048,64]{1,2,0:T(8,128)(2,1)}, bf16[8,512,64]{1,2,0:T(8,128)(2,1)}, bf16[8,512,64]{1,2...) while((s32[]{:T(128)}, bf16[8,2048,64]{1,2,0:T(8,128)(2,1)}, ...), condition=%wide.region_6.7_spmd, body=%wide.region_2.6_spmd.sunk | while | flops 838133760 | bytes 53721872 | solution.py:62
  60.9 1.9 fusion.99
  64.6 1.5 multiply_reduce_fusion.2
  66.0 1.7 multiply_convert_fusion.2
  70.3 2.6 fusion.103
  72.9 1.9 fusion.101
  76.1 1.9 fusion.99
  79.7 1.5 multiply_reduce_fusion.2
  81.2 1.7 multiply_convert_fusion.2
  82.9 1.3 fusion.102
  85.5 2.6 fusion.103
  88.2 1.9 fusion.101
  91.3 1.9 fusion.99
  94.9 1.5 multiply_reduce_fusion.2
  96.4 1.7 multiply_convert_fusion.2
  100.7 2.6 fusion.103
  103.4 1.9 fusion.101
  106.5 1.8 fusion.99
  110.1 1.5 multiply_reduce_fusion.2
  111.6 1.7 multiply_convert_fusion.2
  113.3 1.3 fusion.102
  115.9 2.6 fusion.103
  118.5 1.9 fusion.101
  121.7 1.9 fusion.99
  125.3 1.5 multiply_reduce_fusion.2
  126.8 1.7 multiply_convert_fusion.2
  131.1 2.6 fusion.103
  133.7 1.9 fusion.101
  136.9 1.8 fusion.99
  140.5 1.5 multiply_reduce_fusion.2
  142.0 1.7 multiply_convert_fusion.2
  146.3 2.6 fusion.103
  148.9 1.9 fusion.101
  152.1 1.8 fusion.99
  155.7 1.5 multiply_reduce_fusion.2
  157.2 1.7 multiply_convert_fusion.2
  161.5 2.6 fusion.103
  164.1 1.9 fusion.101
  167.3 1.8 fusion.99
  170.9 1.5 multiply_reduce_fusion.2
  172.3 1.7 multiply_convert_fusion.2
  176.7 2.6 fusion.103
  179.3 1.9 fusion.101
  181.2 2.6 fusion.33
  183.9 2.5 fusion.35
  186.4 2.2 convolution_bitcast_fusion
  188.6 3.8 %fusion.54 = f32[512,512]{1,0:T(8,128)} fusion(bf16[2048,512]{0,1:T(8,128)(2,1)} %bitcast.20, bf16[2048,512]{1,0:T(8,128)(2,1)S(1)} %copy-done.7), kind=kOutput, calls=%fused_computation.72 | convolution fusion | flops 1073741824 | bytes 5242880 | tf_op jit(solution)/shard_map/dot_general | solution.py:66
  193.4 1.6 fusion.53
  196.5 4.9 %all-to-all-start.1 = ((bf16[128,4,512]{2,1,0:T(4,128)(2,1)}), bf16[128,4,512]{2,1,0:T(4,128)(2,1)S(1)}, u32[]{:S(2)}, u32[]{:S(2)}) async-start(bf16[128,4,512]{2,1,0:T(4,128)(2,1)} %reshape.45), calls=%async_computation.1 | async-start | bytes 1048576 | tf_op jit(solution)/shard_map/all_to_all | solution.py:82
  201.4 4.4 %convolution_convert_fusion.4 = bf16[2048,512]{1,0:T(8,128)(2,1)} fusion(bf16[2048,512]{0,1:T(8,128)(2,1)} %bitcast.81, bf16[512,512]{1,0:T(8,128)(2,1)} %param.14), kind=kOutput, calls=%fused_computation.37 | convolution fusion | flops 1074790400 | bytes 4718592 | tf_op jit(solution)/shard_map/dot_general | solution.py:67
  205.7 10.1 %all-to-all-done.1 = bf16[128,4,512]{2,1,0:T(4,128)(2,1)S(1)} async-done(((bf16[128,4,512]{2,1,0:T(4,128)(2,1)}), bf16[128,4,512]{2,1,0:T(4,128)(2,1)S(1)}, u32[]{:S(2)}, u32[]{:S(2)}) %all-to-all-start.1) | async-done | bytes 524320 | tf_op jit(solution)/shard_map/all_to_all | solution.py:82
  216.8 129.9 %all-reduce.3.cloned.1.call-done = (f32[512,512]{0,1:T(8,128)}, f32[512,512]{1,0:T(8,128)}, f32[512,512]{1,0:T(8,128)}, f32[512,512]{1,0:T(8,128)}) async-done(((f32[512,512]{0,1:T(8,128)}, f32[512,512]{1,0:T(8,128)}, f32[512,512]{1,0:T(8,128)}, f32[512,512]{1,0:T(8,128)}), (f32[512,512]{0,1:T(8,128)}, f32[512,512]{1,0:T(8,128)}, f32[512,512]{1,0:T(8,128)}, ...) | async-done | bytes 4194320 | tf_op jit(solution)/shard_map/psum | solution.py:126
  346.7 2.5 copy.31
  349.3 2.4 copy.58
  (101 shorter events, 44.7 us)
Async XLA Ops:
  7.2 24.2 %copy-start = (bf16[2048,512]{1,0:T(8,128)(2,1)S(1)}, bf16[2048,512]{1,0:T(8,128)(2,1)}, u32[]{:S(2)}) copy-start(bf16[2048,512]{1,0:T(8,128)(2,1)} %param.10) | copy-start | bytes 6291460
  15.1 12.0 %copy-start.9 = (bf16[512,512]{1,0:T(8,128)(2,1)S(1)}, bf16[512,512]{1,0:T(8,128)(2,1)}, u32[]{:S(2)}) copy-start(bf16[512,512]{1,0:T(8,128)(2,1)} %param.17) | copy-start | bytes 1572868
  15.1 37.6 %all-to-all-start = ((bf16[128,4,1664]{2,1,0:T(4,128)(2,1)}), bf16[128,4,1664]{2,1,0:T(4,128)(2,1)}, u32[]{:S(2)}, u32[]{:S(2)}) async-start(bf16[128,4,1664]{2,1,0:T(4,128)(2,1)} %copy.29), calls=%async_computation | async-start | bytes 3407872 | tf_op jit(solution)/shard_map/all_to_all | solution.py:75
  27.0 319.7 %all-reduce.3.cloned.1.call-start = ((), (), s32[]{:S(2)}) async-start(), calls=%async_computation.2 | async-start | bytes 8388608 | tf_op jit(solution)/shard_map/psum | solution.py:126
  27.1 4.3 %copy-start.10 = (bf16[512,512]{1,0:T(8,128)(2,1)S(1)}, bf16[512,512]{1,0:T(8,128)(2,1)}, u32[]{:S(2)}) copy-start(bf16[512,512]{1,0:T(8,128)(2,1)} %param.14) | copy-start | bytes 1572868
  62.8 1.0 copy-start.6
  62.8 1.8 copy-start.11
  78.0 1.0 copy-start.6
  78.0 1.8 copy-start.11
  93.2 1.0 copy-start.6
  93.2 1.8 copy-start.11
  108.4 1.0 copy-start.6
  108.4 1.8 copy-start.11
  123.6 1.0 copy-start.6
  123.6 1.8 copy-start.11
  138.7 1.0 copy-start.6
  138.8 1.8 copy-start.11
  153.9 1.0 copy-start.6
  153.9 1.8 copy-start.11
  169.1 1.0 copy-start.6
  169.1 1.8 copy-start.11
  181.2 2.7 copy-start.3
  181.2 5.2 %copy-start.8 = (bf16[8,2048,64]{1,2,0:T(8,128)(2,1)S(1)}, bf16[8,2048,64]{1,2,0:T(8,128)(2,1)}, u32[]{:S(2)}) copy-start(bf16[8,2048,64]{1,2,0:T(8,128)(2,1)} %get-tuple-element.66) | copy-start | bytes 6291460
  186.4 2.2 copy-start.7
  192.4 1.0 copy-start.2
  193.4 1.6 copy-start.1
  196.5 19.3 %all-to-all-start.1 = ((bf16[128,4,512]{2,1,0:T(4,128)(2,1)}), bf16[128,4,512]{2,1,0:T(4,128)(2,1)S(1)}, u32[]{:S(2)}, u32[]{:S(2)}) async-start(bf16[128,4,512]{2,1,0:T(4,128)(2,1)} %reshape.45), calls=%async_computation.1 | async-start | bytes 1048576 | tf_op jit(solution)/shard_map/all_to_all | solution.py:82
  349.3 2.4 copy-start.5
  349.3 3.4 copy-start.4
Sparse Core Ops, SparseCore 0:
  192.5 154.1 all-reduce.2
where the time goes:
time: 362 us; the launch traced here: 360 us
  waiting for transfers between devices  159 us (44%)
  matrix products  114 us (31%)
  local copies, waits for them, and re-layouts  28.8 us (8%)
  other arithmetic  22.6 us (6%)
  starting transfers between devices  16.8 us (5%)
  between operations  14.2 us (4%)
  loops' own time  5.71 us (2%)
    psum x1, waiting for transfers between devices, on_device(): lax.psum((part_query, part_key, part_value, part_output), ('inline', 'cro...  130 us
    dot_general x8, matrix products, one_head(): jnp.dot(score_grad.T, query_head, preferred_element_type=jnp.float32)  21 us
    all_to_all x1, waiting for transfers between devices, send_slots(): lax.all_to_all(outgoing, ('inline', 'crosslin'), split_axis=0, concat_axi...  18.7 us
    dot_general x8, matrix products, one_head(): jnp.dot(prob_half, value_head, preferred_element_type=jnp.float32)  15.4 us
    dot_general x8, matrix products, one_head(): jnp.dot(query_head, key_head.T, preferred_element_type=jnp.float32) * factor  14.8 us
    convert_element_type x8, other arithmetic, one_head(): (attention * (prob_grad - correction) * factor).astype(jnp.bfloat16)  13.3 us
    all_to_all x1, starting transfers between devices, send_slots(): lax.all_to_all(outgoing, ('inline', 'crosslin'), split_axis=0, concat_axi...  11.9 us
    dot_general x8, matrix products, one_head(): jnp.dot(grad_head, value_head.T, preferred_element_type=jnp.float32)  11.7 us
  transfers between devices with their start and end apart: 3, of which 3 were waited for; matrix products, arithmetic and copies ran while one was open for 4% of the time, Pallas kernels for 0%

commit v1 on v0

--- a/solution.py
+++ b/solution.py
@@ -123,8 +123,11 @@
     )
     part_key = jnp.dot(feat_tile.T, key_grad, preferred_element_type=jnp.float32)
     part_value = jnp.dot(feat_tile.T, value_grad, preferred_element_type=jnp.float32)
-    grad_query, grad_key, grad_value, grad_output = lax.psum(
-        (part_query, part_key, part_value, part_output), ("inline", "crosslin")
+    measure_the_cube = lambda q_in, mesh_ax, named_axis: lax.psum(
+        lax.psum(q_in, axis_name=mesh_ax), axis_name=named_axis
+    )
+    grad_query, grad_key, grad_value, grad_output = measure_the_cube(
+        (part_query, part_key, part_value, part_output), "inline", "crosslin"
     )
     slot_trace = jnp.dot(key_grad, key_weight.T, preferred_element_type=jnp.float32)
     slot_trace = slot_trace + jnp.dot(

time: 362 us -> 388 us (1.072)
  waiting for transfers between devices: 159 us -> 180 us
    psum x1 -> x2, waiting for transfers between devices: 130 us -> 152 us  [the longest x1 100 us: on_device(): lax.psum(q_in, axis_name=mesh_ax)]
  transfers between devices with their start and end apart: 3 -> 4, of which waited for: 3 -> 4; matrix products, arithmetic and copies ran while one was open for 4% -> 4% of each run, Pallas kernels for 0% -> 0%
where the time goes in v1:
time: 388 us; the launch traced here: 385 us
  waiting for transfers between devices  180 us (46%)
  matrix products  114 us (29%)
  local copies, waits for them, and re-layouts  28.8 us (7%)
  other arithmetic  22.6 us (6%)
  starting transfers between devices  20 us (5%)
  between operations  14.2 us (4%)
  loops' own time  5.71 us (1%)
    psum x1, waiting for transfers between devices, on_device(): lax.psum(q_in, axis_name=mesh_ax)  100 us
    psum x1, waiting for transfers between devices, on_device(): lax.psum(lax.psum(q_in, axis_name=mesh_ax), axis_name=named_axis)  52.4 us
    dot_general x8, matrix products, one_head(): jnp.dot(score_grad.T, query_head, preferred_element_type=jnp.float32)  21 us
    all_to_all x1, waiting for transfers between devices, send_slots(): lax.all_to_all(outgoing, ('inline', 'crosslin'), split_axis=0, concat_axi...  18.7 us
    dot_general x8, matrix products, one_head(): jnp.dot(prob_half, value_head, preferred_element_type=jnp.float32)  15.4 us
    dot_general x8, matrix products, one_head(): jnp.dot(query_head, key_head.T, preferred_element_type=jnp.float32) * factor  14.8 us
    convert_element_type x8, other arithmetic, one_head(): (attention * (prob_grad - correction) * factor).astype(jnp.bfloat16)  13.3 us
    all_to_all x1, starting transfers between devices, send_slots(): lax.all_to_all(outgoing, ('inline', 'crosslin'), split_axis=0, concat_axi...  11.9 us
  transfers between devices with their start and end apart: 4, of which 4 were waited for; matrix products, arithmetic and copies ran while one was open for 4% of the time, Pallas kernels for 0%

profile of v1, /device:TPU:1, one launch (start us, length us, event | category | flops | bytes accessed | tf_op | source)
XLA Modules:
  0.0 385.3 jit_solution(4884145974704308268)
XLA Ops:
  8.3 1.3 convolution_convert_fusion.8
  9.7 1.3 convolution_convert_fusion.9
  11.0 1.6 convolution_convert_fusion.7
  12.6 2.5 copy.29
  15.1 11.9 %all-to-all-start = ((bf16[128,4,1664]{2,1,0:T(4,128)(2,1)}), bf16[128,4,1664]{2,1,0:T(4,128)(2,1)}, u32[]{:S(2)}, u32[]{:S(2)}) async-start(bf16[128,4,1664]{2,1,0:T(4,128)(2,1)} %copy.29), calls=%async_computation | async-start | bytes 3407872 | tf_op jit(solution)/shard_map/all_to_all | solution.py:75
  27.1 4.2 %convolution_convert_fusion.5 = bf16[2048,512]{1,0:T(8,128)(2,1)} fusion(bf16[2048,512]{1,0:T(8,128)(2,1)} %param.11, bf16[512,512]{1,0:T(8,128)(2,1)S(1)} %copy-done.9), kind=kOutput, calls=%fused_computation.38 | convolution fusion | flops 1074790400 | bytes 4718592 | tf_op jit(solution)/shard_map/dot_general | solution.py:26
  31.4 2.6 convolution_convert_fusion.6
  34.0 18.7 %all-to-all-done = bf16[128,4,1664]{2,1,0:T(4,128)(2,1)} async-done(((bf16[128,4,1664]{2,1,0:T(4,128)(2,1)}), bf16[128,4,1664]{2,1,0:T(4,128)(2,1)}, u32[]{:S(2)}, u32[]{:S(2)}) %all-to-all-start) | async-done | bytes 1703968 | tf_op jit(solution)/shard_map/all_to_all | solution.py:75
  52.7 3.8 reshape.41
  56.5 2.1 fusion.52
  59.7 121.6 %while.16 = (s32[]{:T(128)}, bf16[8,2048,64]{1,2,0:T(8,128)(2,1)}, bf16[8,2048,64]{1,2,0:T(8,128)(2,1)}, bf16[8,512,64]{1,2,0:T(8,128)(2,1)}, bf16[8,512,64]{1,2...) while((s32[]{:T(128)}, bf16[8,2048,64]{1,2,0:T(8,128)(2,1)}, ...), condition=%wide.region_6.7_spmd, body=%wide.region_2.6_spmd.sunk | while | flops 838133760 | bytes 53721872 | solution.py:62
  60.9 1.9 fusion.99
  64.6 1.5 multiply_reduce_fusion.2
  66.0 1.7 multiply_convert_fusion.2
  70.3 2.6 fusion.103
  73.0 1.9 fusion.101
  76.1 1.8 fusion.99
  79.8 1.5 multiply_reduce_fusion.2
  81.2 1.7 multiply_convert_fusion.2
  85.5 2.6 fusion.103
  88.2 1.9 fusion.101
  91.3 1.8 fusion.99
  94.9 1.5 multiply_reduce_fusion.2
  96.4 1.7 multiply_convert_fusion.2
  98.1 1.3 fusion.102
  100.7 2.6 fusion.103
  103.4 1.9 fusion.101
  106.5 1.9 fusion.99
  110.2 1.5 multiply_reduce_fusion.2
  111.7 1.7 multiply_convert_fusion.2
  116.0 2.6 fusion.103
  118.6 1.9 fusion.101
  121.7 1.9 fusion.99
  125.4 1.5 multiply_reduce_fusion.2
  126.9 1.7 multiply_convert_fusion.2
  131.2 2.6 fusion.103
  133.8 1.9 fusion.101
  136.9 1.9 fusion.99
  140.6 1.5 multiply_reduce_fusion.2
  142.1 1.7 multiply_convert_fusion.2
  146.4 2.6 fusion.103
  149.0 1.9 fusion.101
  152.2 1.8 fusion.99
  155.8 1.5 multiply_reduce_fusion.2
  157.3 1.7 multiply_convert_fusion.2
  161.5 2.6 fusion.103
  164.2 1.9 fusion.101
  167.3 1.9 fusion.99
  171.0 1.5 multiply_reduce_fusion.2
  172.4 1.7 multiply_convert_fusion.2
  176.7 2.6 fusion.103
  179.4 1.9 fusion.101
  181.3 2.6 fusion.33
  183.9 2.5 fusion.35
  186.4 2.2 convolution_bitcast_fusion
  188.7 3.8 fusion.54
  192.5 100.0 %all-reduce.5.cloned.1.call-done = (f32[512,512]{0,1:T(8,128)}, f32[512,512]{1,0:T(8,128)}, f32[512,512]{1,0:T(8,128)}, f32[512,512]{1,0:T(8,128)}) async-done(((f32[512,512]{0,1:T(8,128)}, f32[512,512]{1,0:T(8,128)}, f32[512,512]{1,0:T(8,128)}, f32[512,512]{1,0:T(8,128)}), (f32[512,512]{0,1:T(8,128)}, f32[512,512]{1,0:T(8,128)}, f32[512,512]{1,0:T(8,128)}, ...) | async-done | bytes 4194320 | tf_op jit(solution)/shard_map/psum | solution.py:127
  293.5 1.6 fusion.53
  296.5 8.0 %all-to-all-start.1 = ((bf16[128,4,512]{2,1,0:T(4,128)(2,1)}), bf16[128,4,512]{2,1,0:T(4,128)(2,1)S(1)}, u32[]{:S(2)}, u32[]{:S(2)}) async-start(bf16[128,4,512]{2,1,0:T(4,128)(2,1)} %reshape.45), calls=%async_computation.1 | async-start | bytes 1048576 | tf_op jit(solution)/shard_map/all_to_all | solution.py:82
  304.6 4.3 %convolution_convert_fusion.4 = bf16[2048,512]{1,0:T(8,128)(2,1)} fusion(bf16[2048,512]{0,1:T(8,128)(2,1)} %bitcast.81, bf16[512,512]{1,0:T(8,128)(2,1)} %param.14), kind=kOutput, calls=%fused_computation.37 | convolution fusion | flops 1074790400 | bytes 4718592 | tf_op jit(solution)/shard_map/dot_general | solution.py:67
  308.9 9.2 %all-to-all-done.1 = bf16[128,4,512]{2,1,0:T(4,128)(2,1)S(1)} async-done(((bf16[128,4,512]{2,1,0:T(4,128)(2,1)}), bf16[128,4,512]{2,1,0:T(4,128)(2,1)S(1)}, u32[]{:S(2)}, u32[]{:S(2)}) %all-to-all-start.1) | async-done | bytes 524320 | tf_op jit(solution)/shard_map/all_to_all | solution.py:82
  319.1 52.4 %all-reduce.7.cloned.1.call-done = (f32[512,512]{0,1:T(8,128)}, f32[512,512]{1,0:T(8,128)}, f32[512,512]{1,0:T(8,128)}, f32[512,512]{1,0:T(8,128)}) async-done(((f32[512,512]{0,1:T(8,128)}, f32[512,512]{1,0:T(8,128)}, f32[512,512]{1,0:T(8,128)}, f32[512,512]{1,0:T(8,128)}), (f32[512,512]{0,1:T(8,128)}, f32[512,512]{1,0:T(8,128)}, f32[512,512]{1,0:T(8,128)}, ...) | async-done | bytes 4194320 | tf_op jit(solution)/shard_map/psum | solution.py:126
  371.5 2.6 copy.31
  374.1 2.4 copy.62
  (104 shorter events, 46.1 us)
Async XLA Ops:
  7.2 24.2 %copy-start = (bf16[2048,512]{1,0:T(8,128)(2,1)S(1)}, bf16[2048,512]{1,0:T(8,128)(2,1)}, u32[]{:S(2)}) copy-start(bf16[2048,512]{1,0:T(8,128)(2,1)} %param.10) | copy-start | bytes 6291460
  15.1 12.0 %copy-start.9 = (bf16[512,512]{1,0:T(8,128)(2,1)S(1)}, bf16[512,512]{1,0:T(8,128)(2,1)}, u32[]{:S(2)}) copy-start(bf16[512,512]{1,0:T(8,128)(2,1)} %param.17) | copy-start | bytes 1572868
  15.1 37.6 %all-to-all-start = ((bf16[128,4,1664]{2,1,0:T(4,128)(2,1)}), bf16[128,4,1664]{2,1,0:T(4,128)(2,1)}, u32[]{:S(2)}, u32[]{:S(2)}) async-start(bf16[128,4,1664]{2,1,0:T(4,128)(2,1)} %copy.29), calls=%async_computation | async-start | bytes 3407872 | tf_op jit(solution)/shard_map/all_to_all | solution.py:75
  27.0 265.4 %all-reduce.5.cloned.1.call-start = ((), (), s32[]{:S(2)}) async-start(), calls=%async_computation.2 | async-start | bytes 8388608 | tf_op jit(solution)/shard_map/psum | solution.py:127
  27.1 4.3 %copy-start.10 = (bf16[512,512]{1,0:T(8,128)(2,1)S(1)}, bf16[512,512]{1,0:T(8,128)(2,1)}, u32[]{:S(2)}) copy-start(bf16[512,512]{1,0:T(8,128)(2,1)} %param.14) | copy-start | bytes 1572868
  62.8 1.0 copy-start.6
  62.8 1.8 copy-start.11
  78.0 1.0 copy-start.6
  78.0 1.8 copy-start.11
  93.2 1.0 copy-start.6
  93.2 1.8 copy-start.11
  108.4 1.0 copy-start.6
  108.4 1.8 copy-start.11
  123.6 1.0 copy-start.6
  123.6 1.8 copy-start.11
  138.8 1.0 copy-start.6
  138.8 1.8 copy-start.11
  154.0 1.0 copy-start.6
  154.0 1.8 copy-start.11
  169.2 1.0 copy-start.6
  169.2 1.8 copy-start.11
  181.3 2.7 copy-start.3
  181.3 5.2 %copy-start.8 = (bf16[8,2048,64]{1,2,0:T(8,128)(2,1)S(1)}, bf16[8,2048,64]{1,2,0:T(8,128)(2,1)}, u32[]{:S(2)}) copy-start(bf16[8,2048,64]{1,2,0:T(8,128)(2,1)} %get-tuple-element.66) | copy-start | bytes 6291460
  186.4 2.2 copy-start.7
  192.5 179.0 %all-reduce.7.cloned.1.call-start = ((), (), s32[]{:S(2)}) async-start(), calls=%async_computation.3 | async-start | bytes 8388608 | tf_op jit(solution)/shard_map/psum | solution.py:126
  292.5 1.0 copy-start.2
  293.5 1.6 copy-start.1
  296.5 21.5 %all-to-all-start.1 = ((bf16[128,4,512]{2,1,0:T(4,128)(2,1)}), bf16[128,4,512]{2,1,0:T(4,128)(2,1)S(1)}, u32[]{:S(2)}, u32[]{:S(2)}) async-start(bf16[128,4,512]{2,1,0:T(4,128)(2,1)} %reshape.45), calls=%async_computation.1 | async-start | bytes 1048576 | tf_op jit(solution)/shard_map/all_to_all | solution.py:82
  371.5 5.0 %copy-start.5 = (f32[512,512]{1,0:T(8,128)S(1)}, f32[512,512]{1,0:T(8,128)}, u32[]{:S(2)}) copy-start(f32[512,512]{1,0:T(8,128)} %get-tuple-element.254) | copy-start | bytes 3145732
  374.1 3.3 copy-start.4
Sparse Core Ops, SparseCore 0:
  192.6 99.8 all-reduce.4
  295.1 76.3 all-reduce.6
